TPU v7x, 32 devices: a whole 2x2x4 slice. The times are simulated.
32 devices in a mesh: shots: 4 (over x, core), depth: 8 (over z, y).
Axes of the slice: x: 2, y: 2, z: 4, core: 2. Of those that a mesh axis runs over, the one named last changes fastest.
Arguments:
- forward_prev: float32 [4, 64, 128, 256], P('shots', 'depth'), may hold values from -3 to 3
- forward_now: float32 [4, 64, 128, 256], P('shots', 'depth'), may hold values from -3 to 3
- adjoint_prev: float32 [4, 64, 128, 256], P('shots', 'depth'), may hold values from -3 to 3
- adjoint_now: float32 [4, 64, 128, 256], P('shots', 'depth'), may hold values from -3 to 3
- courant: float32 [64, 128, 256], P('depth'), may hold values from 0.05 to 0.18
- wavelet: float32 [2, 512], replicated, may hold values from -5 to 5
- sign_bits: int32 [4, 512], P('shots'), may hold values from 0 to 1
- source_depth: int32 [512], replicated, may hold values from 0 to 63
- source_cell: int32 [512], replicated, may hold values from 0 to 32767
- receiver_depth: int32 [4096], replicated, may hold values from 0 to 63
- receiver_cell: int32 [4096], replicated, may hold values from 0 to 32767
- residual_traces: float32 [4, 2, 4096], P('shots'), may hold values from -5 to 5
Outputs:
- forward_older: float32 [4, 64, 128, 256], P('shots', 'depth')
- forward_newer: float32 [4, 64, 128, 256], P('shots', 'depth')
- adjoint_older: float32 [4, 64, 128, 256], P('shots', 'depth')
- adjoint_newer: float32 [4, 64, 128, 256], P('shots', 'depth')
- gradient: float32 [64, 128, 256], P(None, ('shots', 'depth'))
All inputs are finite; a program needn't handle non-finite values.
Results may differ from a plain program's by a relative error of at most 0.00002.
Values sent between devices are 32-bit elements; how exact they have to be, the bound alone decides.
No kernel may reach another device: no remote copies, remote signals or barrier semaphores. Data moves between devices by JAX's collectives and lax.ppermute only.
A program may use at most 128 MiB of HBM per device.

v0:
```python
import jax
import jax.numpy as jnp
from jax import lax
from jax.sharding import PartitionSpec as P

STEPS = 2
HALO = 4
COEFFS = (-205.0 / 72.0, 8.0 / 5.0, -1.0 / 5.0, 8.0 / 315.0, -1.0 / 560.0)
KERNEL = (1.0 / 16.0, 4.0 / 16.0, 6.0 / 16.0, 4.0 / 16.0, 1.0 / 16.0)


def shifted(values, axis, offset):
    size = values.shape[axis]
    width = abs(offset)
    pads = [(0, 0, 0)] * values.ndim
    if offset > 0:
        kept = lax.slice_in_dim(values, offset, size, axis=axis)
        pads[axis] = (0, width, 0)
    else:
        kept = lax.slice_in_dim(values, 0, size - width, axis=axis)
        pads[axis] = (width, 0, 0)
    return lax.pad(kept, jnp.array(0.0, values.dtype), pads)


def band(size):
    index = jnp.arange(size)
    gap = jnp.abs(index[:, None] - index[None, :])
    matrix = jnp.zeros((size, size), jnp.float32)
    for k in range(1, 5):
        matrix = jnp.where(gap == k, jnp.float32(COEFFS[k]), matrix)
    return matrix


def lateral_laplace(core, zaxis):
    rows, cols = (core.shape[zaxis + 1], core.shape[zaxis + 2])
    high = lax.Precision.HIGHEST
    along_y = jnp.einsum("...xy,yk->...xk", core, band(cols), precision=high)
    along_x = jnp.einsum("...xy,kx->...ky", core, band(rows), precision=high)
    return 3.0 * COEFFS[0] * core + (along_x + along_y)


def depth_laplace(below, core, above, zaxis):
    planes = core.shape[zaxis]
    extended = jnp.concatenate([below, core, above], axis=zaxis)
    total = None
    for k in range(1, 5):
        near = lax.slice_in_dim(
            extended, HALO + k, HALO + k + planes, axis=zaxis
        ) + lax.slice_in_dim(extended, HALO - k, HALO - k + planes, axis=zaxis)
        total = COEFFS[k] * near if total is None else total + COEFFS[k] * near
    return total


def smooth_matrix(size):
    index = jnp.arange(size)
    gap = index[:, None] - index[None, :]
    matrix = jnp.zeros((size, size), jnp.float32)
    for k in range(-2, 3):
        matrix = jnp.where(gap == k, jnp.float32(KERNEL[2 + k]), matrix)
    return matrix


def smooth_lateral(values):
    high = lax.Precision.HIGHEST
    rows, cols = (values.shape[-2], values.shape[-1])
    along_y = jnp.einsum("...xy,yk->...xk", values, smooth_matrix(cols), precision=high)
    return jnp.einsum("...xy,kx->...ky", along_y, smooth_matrix(rows), precision=high)


def smooth(values, axis):
    total = KERNEL[2] * values
    for k in (1, 2):
        total = total + KERNEL[2 + k] * (shifted(values, axis, k) + shifted(values, axis, -k))
    return total


def exchange(fields, dim):
    devices = lax.axis_size("depth")
    length = fields[0].shape[dim]
    up = [(i, i + 1) for i in range(devices - 1)]
    down = [(i + 1, i) for i in range(devices - 1)]
    below, above = ([], [])
    for f in fields:
        below.append(
            lax.ppermute(lax.slice_in_dim(f, length - HALO, length, axis=dim), "depth", up)
        )
        above.append(lax.ppermute(lax.slice_in_dim(f, 0, HALO, axis=dim), "depth", down))
    return (below, above)


def spread(flat, values, first_plane, planes, rows, cols):
    lateral = rows * cols
    limit = planes * lateral
    local = flat - first_plane * lateral
    local = jnp.where((local >= 0) & (local < limit), local, limit)
    grid = jnp.zeros((values.shape[0], limit), jnp.float32).at[:, local].add(values, mode="drop")
    return grid.reshape(values.shape[0], planes, rows, cols)


def spread_dense(depth, cell, values, first_plane, planes, rows, cols):
    steps, count = values.shape
    local = depth - first_plane
    inside = (local >= 0) & (local < planes)
    row_id = jnp.where(inside, local * rows + cell // cols, -1)
    by_row = (row_id[None, :] == jnp.arange(planes * rows)[:, None]).astype(jnp.bfloat16)
    by_col = (cell % cols)[:, None] == jnp.arange(cols)[None, :]
    pieces = []
    rest = values
    for _ in range(3):
        piece = lax.reduce_precision(rest, exponent_bits=8, mantissa_bits=7)
        rest = rest - piece
        pieces.append(piece.astype(jnp.bfloat16))
    stacked = jnp.stack(pieces)
    right = jnp.where(by_col[None, None], stacked[:, :, :, None], jnp.zeros((), jnp.bfloat16))
    right = right.transpose(2, 0, 1, 3).reshape(count, 3 * steps * cols)
    grid = jnp.dot(by_row, right, preferred_element_type=jnp.float32)
    grid = grid.reshape(planes * rows, 3, steps, cols)
    grid = grid[:, 0] + grid[:, 1] + grid[:, 2]
    return grid.transpose(1, 0, 2).reshape(steps, planes, rows, cols)


def reduce_shots(values, dim):
    devices = lax.axis_size("shots")
    me = lax.axis_index("shots")
    length = values.shape[dim]
    shape = values.shape
    blocks = values.reshape(shape[:dim] + (devices, length // devices) + shape[dim + 1 :])
    bit = 1
    while bit < devices:
        count = blocks.shape[dim]
        paired = blocks.reshape(shape[:dim] + (count // 2, 2, length // devices) + shape[dim + 1 :])
        mine = me // bit % 2
        keep = lax.dynamic_index_in_dim(paired, mine, axis=dim + 1, keepdims=False)
        send = lax.dynamic_index_in_dim(paired, 1 - mine, axis=dim + 1, keepdims=False)
        pairs = [(i, i ^ bit) for i in range(devices)]
        blocks = keep + lax.ppermute(send, "shots", pairs)
        bit *= 2
    return blocks.reshape(shape[:dim] + (length // devices,) + shape[dim + 1 :])


def on_device(
    forward_prev,
    forward_now,
    adjoint_prev,
    adjoint_now,
    courant,
    wavelet,
    sign_bits,
    source_depth,
    source_cell,
    receiver_depth,
    receiver_cell,
    residual_traces,
):
    planes, rows, cols = courant.shape
    lateral = rows * cols
    source_flat = source_depth * lateral + source_cell
    receiver_flat = receiver_depth * lateral + receiver_cell
    signs = (2 * sign_bits - 1).astype(jnp.float32)
    position = lax.axis_index("depth")
    earlier = [forward_prev, adjoint_prev]
    current = [forward_now, adjoint_now]
    zaxis = 1
    below, above = exchange(current, zaxis)
    first_plane = position * planes
    correlation = None
    forward_terms = spread_dense(
        source_depth, source_cell, signs[0][None, :] * wavelet, first_plane, planes, rows, cols
    )
    adjoint_terms = spread_dense(
        receiver_depth, receiver_cell, residual_traces[0], first_plane, planes, rows, cols
    )
    markers = []
    for step in range(STEPS):
        terms = [forward_terms[step : step + 1], adjoint_terms[step : step + 1]]
        if markers:
            _, current[1] = lax.optimization_barrier((markers[1], current[1]))
        partial = lax.optimization_barrier(
            [
                2.0 * current[i]
                - earlier[i]
                + courant * lateral_laplace(current[i], zaxis)
                + terms[i]
                for i in range(2)
            ]
        )
        fresh = []
        halos = ([], [])
        markers = []
        for i in range(2):
            if i > 0 and step + 1 < STEPS:
                _, below[i], above[i] = lax.optimization_barrier((markers[0], below[i], above[i]))
            fresh.append(
                partial[i] + courant * depth_laplace(below[i], current[i], above[i], zaxis)
            )
            if step + 1 < STEPS:
                devices = lax.axis_size("depth")
                length = fresh[i].shape[zaxis]
                marker = lax.ppermute(
                    lax.slice_in_dim(fresh[i], length - 1, length, axis=zaxis),
                    "depth",
                    [(j, j + 1) for j in range(devices - 1)],
                )
                rest = lax.ppermute(
                    lax.slice_in_dim(fresh[i], length - HALO, length - 1, axis=zaxis),
                    "depth",
                    [(j, j + 1) for j in range(devices - 1)],
                )
                leading = lax.ppermute(
                    lax.slice_in_dim(fresh[i], 0, HALO, axis=zaxis),
                    "depth",
                    [(j + 1, j) for j in range(devices - 1)],
                )
                halos[0].append(jnp.concatenate([rest, marker], axis=zaxis))
                halos[1].append(leading)
                markers.append(marker)
        if step + 1 < STEPS:
            below, above = halos
        part = fresh[0][0] * fresh[1][0]
        correlation = part if correlation is None else correlation + part
        earlier, current = (current, fresh)
    lateral_smooth = smooth_lateral(correlation)
    reduced = reduce_shots(lateral_smooth, 1)
    columns = lax.all_to_all(reduced, "depth", split_axis=1, concat_axis=0, tiled=True)
    gradient = smooth(columns, 0)
    return (earlier[0], current[0], earlier[1], current[1], gradient)


def solution(mesh):
    in_specs = (
        P("shots", "depth", None, None),
        P("shots", "depth", None, None),
        P("shots", "depth", None, None),
        P("shots", "depth", None, None),
        P("depth", None, None),
        P(),
        P("shots", None),
        P(),
        P(),
        P(),
        P(),
        P("shots", None, None),
    )
    out_specs = (
        P("shots", "depth", None, None),
        P("shots", "depth", None, None),
        P("shots", "depth", None, None),
        P("shots", "depth", None, None),
        P(None, ("shots", "depth"), None),
    )
    return jax.shard_map(
        on_device, mesh=mesh, in_specs=in_specs, out_specs=out_specs, check_vma=False
    )
```

profile of v0, /device:TPU:0, one launch (start us, length us, event | category | flops | bytes accessed | tf_op | source)
XLA Modules:
  0.0 128.9 jit_solution(12188059574222061292)
XLA Ops:
  0.6 2.4 %fusion.274 = (f32[1,4,128,256]{3,2,1,0:T(8,128)}, f32[1,4,128,256]{3,2,1,0:T(8,128)}) fusion(f32[1,8,128,256]{3,2,1,0:T(8,128)} %param.13), kind=kLoop, calls=%fused_computation.348 | loop fusion | bytes 2097152 | tf_op jit(solution)/shard_map/slice | solution.py:87
  3.0 5.7 %collective-permute-start.1 = (f32[1,4,128,256]{3,2,1,0:T(8,128)}, f32[1,4,128,256]{3,2,1,0:T(8,128)}, u32[]{:S(2)}, u32[]{:S(2)}) collective-permute-start(f32[1,4,128,256]{3,2,1,0:T(8,128)} %get-tuple-element.37), channel_id=1, source_target_pairs={{0,1},{1,2},{2,3},{3,4},{4,5},{5,6},{6,7},{8,9},{9,10},{10,11},{11... | collective-permute-start | bytes 1572872 | tf_op jit(solution)/shard_map/ppermute | solution.py:85
  8.7 1.3 collective-permute-start
  11.1 5.5 %collective-permute-start.3 = (f32[1,4,128,256]{3,2,1,0:T(8,128)}, f32[1,4,128,256]{3,2,1,0:T(8,128)}, u32[]{:S(2)}, u32[]{:S(2)}) collective-permute-start(f32[1,4,128,256]{3,2,1,0:T(8,128)} %get-tuple-element.35), channel_id=1, source_target_pairs={{0,1},{1,2},{2,3},{3,4},{4,5},{5,6},{6,7},{8,9},{9,10},{10,11},{11... | collective-permute-start | bytes 1572872 | tf_op jit(solution)/shard_map/ppermute | solution.py:85
  16.6 1.3 collective-permute-start.4
  17.9 2.0 %convolution_bitcast_fusion.4 = f32[1,8,128,256]{3,2,1,0:T(8,128)} fusion(f32[1,8,128,256]{3,2,1,0:T(8,128)S(1)} %copy-done.5), kind=kOutput, calls=%fused_computation.33 | convolution fusion | flops 805961728 | bytes 2097152 | tf_op jit(solution)/shard_map/...xy,yk->...xk/dot_general | solution.py:37
  20.7 13.2 %fusion.1 = f32[1024,3,2,256]{3,0,2,1:T(8,128)S(1)} fusion(pred[4096,256]{0,1:T(8,128)(4,1)S(1)} %iota_compare_fusion.1, s32[4096]{0:T(1024)S(1)} %get-tuple-element.47, bf16[4096,3,2]{0,2,1:T(2,128)(2,1)S(1)} %maximum_bitcast_fusion), kind=kOutput, calls=%fused_computation.2 | convolution fusion | flops 12895387648 | bytes 7405568 | tf_op jit(solution)/shard_map/dot_general | solution.py:116
  35.8 1.8 %fusion.12 = f32[1024,3,2,256]{3,0,2,1:T(8,128)S(1)} fusion(pred[512,256]{0,1:T(8,128)(4,1)S(1)} %iota_compare_fusion.3, s32[512]{0:T(512)S(1)} %get-tuple-element.52, bf16[512,3,2]{0,2,1:T(2,128)(2,1)S(1)} %maximum_bitcast_fusion.1), kind=kOutput, calls=%fused_computation.21 | convolution fusion | flops 1611923456 | bytes 6430720 | tf_op jit(solution)/shard_map/dot_general | solution.py:116
  40.3 2.4 %fusion.26 = f32[1,8,128,256]{3,2,1,0:T(8,128)} fusion(f32[1,8,128,256]{3,2,1,0:T(8,128)S(1)} %bitcast.208, f32[1,8,128,256]{3,2,1,0:T(8,128)S(1)} %copy-done.9, f32[1,8,128,256]{3,2,1,0:T(8,128)S(1)} %copy-done.5, f32[8,128,256]{2,1,0:T(8,128)S(1)} %copy-done, f32[1,8,128,256]{3,2,1,0:T(8,128)S(1)} %copy-done.14), kind=kOutput, calls=%fused_computation.46 | convolution fusion | flops 404914176 | bytes 6291456 | tf_op jit(solution)/shard_map/...xy,kx->...ky/dot_general | solution.py:38
  43.9 2.4 %fusion.21 = f32[1,8,128,256]{3,2,1,0:T(8,128)} fusion(f32[1,8,128,256]{3,2,1,0:T(8,128)S(1)} %bitcast.209, f32[1,8,128,256]{3,2,1,0:T(8,128)S(1)} %convolution_bitcast_fusion.6, f32[1,8,128,256]{3,2,1,0:T(8,128)S(1)} %copy-done.3, f32[8,128,256]{2,1,0:T(8,128)S(1)} %copy-done, f32[1,8,128,256]{3,2,1,0:T(8,128)S(1)} %copy-done.15), kind=kOutput, calls=%fused_computation.41 | convolution fusion | flops 404914176 | bytes 6291456 | tf_op jit(solution)/shard_map/...xy,kx->...ky/dot_general | solution.py:38
  49.4 4.7 %collective-permute-start.2 = (f32[1,1,128,256]{3,2,1,0:T(8,128)S(1)}, f32[1,1,128,256]{3,2,1,0:T(8,128)S(1)}, u32[]{:S(2)}, u32[]{:S(2)}) collective-permute-start(f32[1,1,128,256]{3,2,1,0:T(8,128)S(1)} %slice.289), channel_id=1, source_target_pairs={{0,1},{1,2},{2,3},{3,4},{4,5},{5,6},{6,7},{8,9},{9,10},{10,11},{11... | collective-permute-start | bytes 393224 | tf_op jit(solution)/shard_map/ppermute | solution.py:199
  54.1 3.7 %collective-permute-start.7 = (f32[1,3,128,256]{3,2,1,0:T(8,128)S(1)}, f32[1,3,128,256]{3,2,1,0:T(8,128)S(1)}, u32[]{:S(2)}, u32[]{:S(2)}) collective-permute-start(f32[1,3,128,256]{3,2,1,0:T(8,128)S(1)} %slice.305), channel_id=1, source_target_pairs={{0,1},{1,2},{2,3},{3,4},{4,5},{5,6},{6,7},{8,9},{9,10},{10,11},{11... | collective-permute-start | bytes 1179656 | tf_op jit(solution)/shard_map/ppermute | solution.py:204
  57.8 1.3 %collective-permute-start.6 = (f32[1,4,128,256]{3,2,1,0:T(8,128)S(1)}, f32[1,4,128,256]{3,2,1,0:T(8,128)S(1)}, u32[]{:S(2)}, u32[]{:S(2)}) collective-permute-start(f32[1,4,128,256]{3,2,1,0:T(8,128)S(1)} %slice.300), channel_id=1, source_target_pairs={{1,0},{2,1},{3,2},{4,3},{5,4},{6,5},{7,6},{9,8},{10,9},{11,10},{12... | collective-permute-start | bytes 1572872 | tf_op jit(solution)/shard_map/ppermute | solution.py:209
  63.2 4.7 %collective-permute-start.5 = (f32[1,1,128,256]{3,2,1,0:T(8,128)S(1)}, f32[1,1,128,256]{3,2,1,0:T(8,128)S(1)}, u32[]{:S(2)}, u32[]{:S(2)}) collective-permute-start(f32[1,1,128,256]{3,2,1,0:T(8,128)S(1)} %slice.298), channel_id=1, source_target_pairs={{0,1},{1,2},{2,3},{3,4},{4,5},{5,6},{6,7},{8,9},{9,10},{10,11},{11... | collective-permute-start | bytes 393224 | tf_op jit(solution)/shard_map/ppermute | solution.py:199
  67.9 1.4 %fusion.31 = f32[1,8,128,256]{3,2,1,0:T(8,128)S(1)} fusion(f32[1,8,128,256]{3,2,1,0:T(8,128)S(1)} %bitcast.207, f32[1,8,128,256]{3,2,1,0:T(8,128)S(1)} %convolution_bitcast_fusion.2, f32[1,8,128,256]{3,2,1,0:T(8,128)S(1)} %fusion.70, f32[8,128,256]{2,1,0:T(8,128)S(1)} %copy-done, f32[1,8,128,256]{3,2,1,0:T(8,128)S(1)} %copy-done.4), kind=kOutput, calls=%fused_computation.51 | convolution fusion | flops 404914176 | bytes 6291456 | tf_op jit(solution)/shard_map/...xy,kx->...ky/dot_general | solution.py:38
  69.4 3.1 %collective-permute-start.9 = (f32[1,3,128,256]{3,2,1,0:T(8,128)S(1)}, f32[1,3,128,256]{3,2,1,0:T(8,128)S(1)}, u32[]{:S(2)}, u32[]{:S(2)}) collective-permute-start(f32[1,3,128,256]{3,2,1,0:T(8,128)S(1)} %slice.314), channel_id=1, source_target_pairs={{0,1},{1,2},{2,3},{3,4},{4,5},{5,6},{6,7},{8,9},{9,10},{10,11},{11... | collective-permute-start | bytes 1179656 | tf_op jit(solution)/shard_map/ppermute | solution.py:204
  72.4 1.5 %collective-permute-start.8 = (f32[1,4,128,256]{3,2,1,0:T(8,128)S(1)}, f32[1,4,128,256]{3,2,1,0:T(8,128)S(1)}, u32[]{:S(2)}, u32[]{:S(2)}) collective-permute-start(f32[1,4,128,256]{3,2,1,0:T(8,128)S(1)} %slice.311), channel_id=1, source_target_pairs={{1,0},{2,1},{3,2},{4,3},{5,4},{6,5},{7,6},{9,8},{10,9},{11,10},{12... | collective-permute-start | bytes 1572872 | tf_op jit(solution)/shard_map/ppermute | solution.py:209
  74.0 18.6 %collective-permute-done.5 = f32[1,1,128,256]{3,2,1,0:T(8,128)S(1)} collective-permute-done((f32[1,1,128,256]{3,2,1,0:T(8,128)S(1)}, f32[1,1,128,256]{3,2,1,0:T(8,128)S(1)}, u32[]{:S(2)}, u32[]{:S(2)}) %collective-permute-start.5) | collective-permute-done | bytes 131104 | tf_op jit(solution)/shard_map/ppermute | solution.py:199
  93.6 1.4 %fusion.87 = f32[1,8,128,256]{3,2,1,0:T(8,128)S(1)} fusion(f32[1,8,128,256]{3,2,1,0:T(8,128)S(1)} %bitcast.206, f32[8,128,256]{2,1,0:T(8,128)S(1)} %copy-done, f32[1,8,128,256]{3,2,1,0:T(8,128)S(1)} %fusion.61, f32[1,8,128,256]{3,2,1,0:T(8,128)S(1)} %copy-done.6, f32[1,8,128,256]{3,2,1,0:T(8,128)S(1)} %convolution_bitcast_fusion), kind=kOutput, calls=%fused_computation.125 | convolution fusion | flops 404914176 | bytes 6291456 | tf_op jit(solution)/shard_map/...xy,kx->...ky/dot_general | solution.py:38
  95.1 3.5 %collective-permute-done.9 = f32[1,3,128,256]{3,2,1,0:T(8,128)S(1)} collective-permute-done((f32[1,3,128,256]{3,2,1,0:T(8,128)S(1)}, f32[1,3,128,256]{3,2,1,0:T(8,128)S(1)}, u32[]{:S(2)}, u32[]{:S(2)}) %collective-permute-start.9) | collective-permute-done | bytes 393248 | tf_op jit(solution)/shard_map/ppermute | solution.py:204
  103.0 1.9 %collective-permute-done.10 = f32[8,2,32,256]{3,0,2,1:T(8,128)S(1)} collective-permute-done((f32[8,2,32,256]{3,0,2,1:T(8,128)S(1)}, f32[8,2,32,256]{3,0,2,1:T(8,128)S(1)}, u32[]{:S(2)}, u32[]{:S(2)}) %collective-permute-start.10) | collective-permute-done | bytes 524320 | tf_op jit(solution)/shard_map/ppermute | solution.py:136
  105.2 1.6 %collective-permute-start.11 = (f32[8,1,32,256]{3,0,2,1:T(8,128)S(1)}, f32[8,1,32,256]{3,0,2,1:T(8,128)S(1)}, u32[]{:S(2)}, u32[]{:S(2)}) collective-permute-start(f32[8,1,32,256]{3,0,2,1:T(8,128)S(1)} %constant_dynamic-slice_fusion), channel_id=1, source_target_pairs={{0,16},{8,24},{16,0},{24,8},{1,17},{9,25},{17,1},{25,9},{2,18},{10... | collective-permute-start | bytes 786440 | tf_op jit(solution)/shard_map/ppermute | solution.py:136
  106.8 6.9 %collective-permute-done.11 = f32[8,1,32,256]{3,0,2,1:T(8,128)S(1)} collective-permute-done((f32[8,1,32,256]{3,0,2,1:T(8,128)S(1)}, f32[8,1,32,256]{3,0,2,1:T(8,128)S(1)}, u32[]{:S(2)}, u32[]{:S(2)}) %collective-permute-start.11) | collective-permute-done | bytes 262176 | tf_op jit(solution)/shard_map/ppermute | solution.py:136
  113.7 14.1 %all_to_all.18 = f32[8,32,256]{2,0,1:T(8,128)S(1)} all-to-all(f32[8,32,256]{2,0,1:T(8,128)S(1)} %add_bitcast_fusion), channel_id=1, replica_groups=mesh['shots'=4,'depth'=8] {'depth'}, dimensions={1} | all-to-all | bytes 524288 | tf_op jit(solution)/shard_map/all_to_all | solution.py:224
  (105 shorter events, 21.5 us)
Async XLA Ops:
  0.6 9.3 %copy-start.5 = (f32[1,8,128,256]{3,2,1,0:T(8,128)S(1)}, f32[1,8,128,256]{3,2,1,0:T(8,128)}, u32[]{:S(2)}) copy-start(f32[1,8,128,256]{3,2,1,0:T(8,128)} %param.15) | copy-start | bytes 3145732
  3.0 43.3 %collective-permute-start.1 = (f32[1,4,128,256]{3,2,1,0:T(8,128)}, f32[1,4,128,256]{3,2,1,0:T(8,128)}, u32[]{:S(2)}, u32[]{:S(2)}) collective-permute-start(f32[1,4,128,256]{3,2,1,0:T(8,128)} %get-tuple-element.37), channel_id=1, source_target_pairs={{0,1},{1,2},{2,3},{3,4},{4,5},{5,6},{6,7},{8,9},{9,10},{10,11},{11... | collective-permute-start | bytes 1572872 | tf_op jit(solution)/shard_map/ppermute | solution.py:85
  8.7 38.9 %collective-permute-start = (f32[1,4,128,256]{3,2,1,0:T(8,128)}, f32[1,4,128,256]{3,2,1,0:T(8,128)}, u32[]{:S(2)}, u32[]{:S(2)}) collective-permute-start(f32[1,4,128,256]{3,2,1,0:T(8,128)} %get-tuple-element.36), channel_id=1, source_target_pairs={{1,0},{2,1},{3,2},{4,3},{5,4},{6,5},{7,6},{9,8},{10,9},{11,10},{12... | collective-permute-start | bytes 1572872 | tf_op jit(solution)/shard_map/ppermute | solution.py:87
  11.1 8.8 %copy-start.16 = (f32[1,2,4096]{2,1,0:T(2,128)S(1)}, f32[1,2,4096]{2,1,0:T(2,128)}, u32[]{:S(2)}) copy-start(f32[1,2,4096]{2,1,0:T(2,128)} %param.23) | copy-start | bytes 98308
  11.1 8.8 %copy-start.17 = (s32[4096]{0:T(1024)S(1)}, s32[4096]{0:T(1024)}, u32[]{:S(2)}) copy-start(s32[4096]{0:T(1024)} %param.22) | copy-start | bytes 49156
  11.1 8.8 %copy-start.18 = (s32[4096]{0:T(1024)S(1)}, s32[4096]{0:T(1024)}, u32[]{:S(2)}) copy-start(s32[4096]{0:T(1024)} %param.21) | copy-start | bytes 49156
  11.1 49.0 %collective-permute-start.3 = (f32[1,4,128,256]{3,2,1,0:T(8,128)}, f32[1,4,128,256]{3,2,1,0:T(8,128)}, u32[]{:S(2)}, u32[]{:S(2)}) collective-permute-start(f32[1,4,128,256]{3,2,1,0:T(8,128)} %get-tuple-element.35), channel_id=1, source_target_pairs={{0,1},{1,2},{2,3},{3,4},{4,5},{5,6},{6,7},{8,9},{9,10},{10,11},{11... | collective-permute-start | bytes 1572872 | tf_op jit(solution)/shard_map/ppermute | solution.py:85
  16.6 43.5 %collective-permute-start.4 = (f32[1,4,128,256]{3,2,1,0:T(8,128)}, f32[1,4,128,256]{3,2,1,0:T(8,128)}, u32[]{:S(2)}, u32[]{:S(2)}) collective-permute-start(f32[1,4,128,256]{3,2,1,0:T(8,128)} %get-tuple-element.34), channel_id=1, source_target_pairs={{1,0},{2,1},{3,2},{4,3},{5,4},{6,5},{7,6},{9,8},{10,9},{11,10},{12... | collective-permute-start | bytes 1572872 | tf_op jit(solution)/shard_map/ppermute | solution.py:87
  38.1 2.2 %copy-start.14 = (f32[1,8,128,256]{3,2,1,0:T(8,128)S(1)}, f32[1,8,128,256]{3,2,1,0:T(8,128)}, u32[]{:S(2)}) copy-start(f32[1,8,128,256]{3,2,1,0:T(8,128)} %param.14) | copy-start | bytes 3145732
  40.3 2.4 %copy-start.3 = (f32[1,8,128,256]{3,2,1,0:T(8,128)S(1)}, f32[1,8,128,256]{3,2,1,0:T(8,128)}, u32[]{:S(2)}) copy-start(f32[1,8,128,256]{3,2,1,0:T(8,128)} %param.13) | copy-start | bytes 3145732
  49.3 50.7 %copy-start.2 = (f32[1,8,128,256]{3,2,1,0:T(8,128)}, f32[1,8,128,256]{3,2,1,0:T(8,128)S(1)}, u32[]{:S(2)}) copy-start(f32[1,8,128,256]{3,2,1,0:T(8,128)S(1)} %fusion.70) | copy-start | bytes 3145732
  49.4 11.8 %copy-start.6 = (f32[1,8,128,256]{3,2,1,0:T(8,128)S(1)}, f32[1,8,128,256]{3,2,1,0:T(8,128)}, u32[]{:S(2)}) copy-start(f32[1,8,128,256]{3,2,1,0:T(8,128)} %param.15) | copy-start | bytes 3145732
  49.4 10.7 %collective-permute-start.2 = (f32[1,1,128,256]{3,2,1,0:T(8,128)S(1)}, f32[1,1,128,256]{3,2,1,0:T(8,128)S(1)}, u32[]{:S(2)}, u32[]{:S(2)}) collective-permute-start(f32[1,1,128,256]{3,2,1,0:T(8,128)S(1)} %slice.289), channel_id=1, source_target_pairs={{0,1},{1,2},{2,3},{3,4},{4,5},{5,6},{6,7},{8,9},{9,10},{10,11},{11... | collective-permute-start | bytes 393224 | tf_op jit(solution)/shard_map/ppermute | solution.py:199
  54.1 40.9 %collective-permute-start.7 = (f32[1,3,128,256]{3,2,1,0:T(8,128)S(1)}, f32[1,3,128,256]{3,2,1,0:T(8,128)S(1)}, u32[]{:S(2)}, u32[]{:S(2)}) collective-permute-start(f32[1,3,128,256]{3,2,1,0:T(8,128)S(1)} %slice.305), channel_id=1, source_target_pairs={{0,1},{1,2},{2,3},{3,4},{4,5},{5,6},{6,7},{8,9},{9,10},{10,11},{11... | collective-permute-start | bytes 1179656 | tf_op jit(solution)/shard_map/ppermute | solution.py:204
  57.8 41.2 %collective-permute-start.6 = (f32[1,4,128,256]{3,2,1,0:T(8,128)S(1)}, f32[1,4,128,256]{3,2,1,0:T(8,128)S(1)}, u32[]{:S(2)}, u32[]{:S(2)}) collective-permute-start(f32[1,4,128,256]{3,2,1,0:T(8,128)S(1)} %slice.300), channel_id=1, source_target_pairs={{1,0},{2,1},{3,2},{4,3},{5,4},{6,5},{7,6},{9,8},{10,9},{11,10},{12... | collective-permute-start | bytes 1572872 | tf_op jit(solution)/shard_map/ppermute | solution.py:209
  62.6 5.3 %copy-start.4 = (f32[1,8,128,256]{3,2,1,0:T(8,128)S(1)}, f32[1,8,128,256]{3,2,1,0:T(8,128)}, u32[]{:S(2)}) copy-start(f32[1,8,128,256]{3,2,1,0:T(8,128)} %param.13) | copy-start | bytes 3145732
  62.6 5.3 %copy-start.11 = (f32[1,1024,256]{2,1,0:T(8,128)S(1)}, f32[1,1024,256]{2,1,0:T(8,128)}, u32[]{:S(2)}) copy-start(f32[1,1024,256]{2,1,0:T(8,128)} %get-tuple-element.26) | copy-start | bytes 3145732
  63.2 36.8 %copy-start.1 = (f32[1,8,128,256]{3,2,1,0:T(8,128)}, f32[1,8,128,256]{3,2,1,0:T(8,128)S(1)}, u32[]{:S(2)}) copy-start(f32[1,8,128,256]{3,2,1,0:T(8,128)S(1)} %fusion.61) | copy-start | bytes 3145732
  63.2 29.4 %collective-permute-start.5 = (f32[1,1,128,256]{3,2,1,0:T(8,128)S(1)}, f32[1,1,128,256]{3,2,1,0:T(8,128)S(1)}, u32[]{:S(2)}, u32[]{:S(2)}) collective-permute-start(f32[1,1,128,256]{3,2,1,0:T(8,128)S(1)} %slice.298), channel_id=1, source_target_pairs={{0,1},{1,2},{2,3},{3,4},{4,5},{5,6},{6,7},{8,9},{9,10},{10,11},{11... | collective-permute-start | bytes 393224 | tf_op jit(solution)/shard_map/ppermute | solution.py:199
  69.3 24.3 %copy-start.10 = (f32[1,1024,256]{2,1,0:T(8,128)S(1)}, f32[1,1024,256]{2,1,0:T(8,128)}, u32[]{:S(2)}) copy-start(f32[1,1024,256]{2,1,0:T(8,128)} %get-tuple-element.24) | copy-start | bytes 3145732
  69.4 29.3 %collective-permute-start.9 = (f32[1,3,128,256]{3,2,1,0:T(8,128)S(1)}, f32[1,3,128,256]{3,2,1,0:T(8,128)S(1)}, u32[]{:S(2)}, u32[]{:S(2)}) collective-permute-start(f32[1,3,128,256]{3,2,1,0:T(8,128)S(1)} %slice.314), channel_id=1, source_target_pairs={{0,1},{1,2},{2,3},{3,4},{4,5},{5,6},{6,7},{8,9},{9,10},{10,11},{11... | collective-permute-start | bytes 1179656 | tf_op jit(solution)/shard_map/ppermute | solution.py:204
  72.4 27.0 %collective-permute-start.8 = (f32[1,4,128,256]{3,2,1,0:T(8,128)S(1)}, f32[1,4,128,256]{3,2,1,0:T(8,128)S(1)}, u32[]{:S(2)}, u32[]{:S(2)}) collective-permute-start(f32[1,4,128,256]{3,2,1,0:T(8,128)S(1)} %slice.311), channel_id=1, source_target_pairs={{1,0},{2,1},{3,2},{4,3},{5,4},{6,5},{7,6},{9,8},{10,9},{11,10},{12... | collective-permute-start | bytes 1572872 | tf_op jit(solution)/shard_map/ppermute | solution.py:209
  102.9 2.0 %collective-permute-start.10 = (f32[8,2,32,256]{3,0,2,1:T(8,128)S(1)}, f32[8,2,32,256]{3,0,2,1:T(8,128)S(1)}, u32[]{:S(2)}, u32[]{:S(2)}) collective-permute-start(f32[8,2,32,256]{3,0,2,1:T(8,128)S(1)} %bitcast.212), channel_id=1, source_target_pairs={{0,8},{8,0},{16,24},{24,16},{1,9},{9,1},{17,25},{25,17},{2,10},{10... | collective-permute-start | bytes 1572872 | tf_op jit(solution)/shard_map/ppermute | solution.py:136
  105.2 8.4 %collective-permute-start.11 = (f32[8,1,32,256]{3,0,2,1:T(8,128)S(1)}, f32[8,1,32,256]{3,0,2,1:T(8,128)S(1)}, u32[]{:S(2)}, u32[]{:S(2)}) collective-permute-start(f32[8,1,32,256]{3,0,2,1:T(8,128)S(1)} %constant_dynamic-slice_fusion), channel_id=1, source_target_pairs={{0,16},{8,24},{16,0},{24,8},{1,17},{9,25},{17,1},{25,9},{2,18},{10... | collective-permute-start | bytes 786440 | tf_op jit(solution)/shard_map/ppermute | solution.py:136
  (11 other events, 14.2 us)
where the time goes:
time: 130 us; the launch traced here: 129 us
  starting transfers between devices  34.3 us (26%)
  waiting for transfers between devices  30.9 us (24%)
  matrix products  29.6 us (23%)
  local copies, waits for them, and re-layouts  14.2 us (11%)
  blocking collectives  14.1 us (11%)
  other arithmetic  4.42 us (3%)
  between operations  1.4 us (1%)
    ppermute x2, waiting for transfers between devices, on_device(): lax.ppermute(lax.slice_in_dim(fresh[i], length - 1, length, axis=zaxis),...  18.6 us
    dot_general x2, matrix products, spread_dense(): grid = jnp.dot(by_row, right, preferred_element_type=jnp.float32)  15 us
    all_to_all x1, blocking collectives, on_device(): lax.all_to_all(reduced, 'depth', split_axis=1, concat_axis=0, tiled=True)  14.1 us
    ppermute x2, starting transfers between devices, exchange(): lax.ppermute(lax.slice_in_dim(f, length - HALO, length, axis=dim), 'depth...  11.2 us
    ppermute x2, starting transfers between devices, on_device(): lax.ppermute(lax.slice_in_dim(fresh[i], length - 1, length, axis=zaxis),...  9.38 us
    ppermute x2, waiting for transfers between devices, reduce_shots(): blocks = keep + lax.ppermute(send, 'shots', pairs)  8.71 us
    dot_general x4, matrix products, lateral_laplace(): along_x = jnp.einsum('...xy,kx->...ky', core, band(rows), precision=high)  7.44 us
    ppermute x2, starting transfers between devices, on_device(): lax.ppermute(lax.slice_in_dim(fresh[i], length - HALO, length - 1, axis=z...  6.72 us
  transfers between devices with their start and end apart: 12, of which 4 were waited for; matrix products, arithmetic and copies ran while one was open for 31% of the time, Pallas kernels for 0%

commit v1 on v0

--- a/solution.py
+++ b/solution.py
@@ -1,12 +1,51 @@
+import functools
 import jax
 import jax.numpy as jnp
 from jax import lax
 from jax.sharding import PartitionSpec as P
+from jax.lax import axis_index, axis_size, ppermute
 
 STEPS = 2
 HALO = 4
 COEFFS = (-205.0 / 72.0, 8.0 / 5.0, -1.0 / 5.0, 8.0 / 315.0, -1.0 / 560.0)
 KERNEL = (1.0 / 16.0, 4.0 / 16.0, 6.0 / 16.0, 4.0 / 16.0, 1.0 / 16.0)
+
+
+def _lift_signs(packet, axis_k, frame):
+    long_array, block_next = (packet.shape[:axis_k], packet.shape[axis_k + 1 :])
+    built = packet.reshape(*long_array, frame, -1, *block_next)
+    kept_arr = jnp.moveaxis(built, axis_k, 0)
+    return kept_arr
+
+
+def treat_the_figure(body, join_dim):
+    body = jnp.moveaxis(body, 0, join_dim)
+    latest = body.shape
+    f_next = body.reshape(
+        *latest[:join_dim], latest[join_dim] * latest[join_dim + 1], *latest[join_dim + 2 :]
+    )
+    return f_next
+
+
+def follow_side(local_block, named_axis, message, m):
+    y1 = axis_size(named_axis)
+    b_now = axis_index(named_axis)
+    outer, extra = (y1, b_now)
+    g_now = _lift_signs(local_block, message, outer)
+    crops = [g_now[extra]]
+    dev = 1
+    while dev < outer:
+        current_arr = g_now[extra ^ dev]
+        carry_out = ppermute(current_arr, named_axis, perm=[(u, u ^ dev) for u in range(outer)])
+        crops.append(carry_out)
+        dev = dev + 1
+    tall = jnp.stack(crops)
+    g_now = tall[extra ^ jnp.arange(outer)]
+    mid_arr = treat_the_figure(g_now, m)
+    return mid_arr
+
+
+proceed_the_inputs = functools.partial(follow_side, named_axis="depth", message=1, m=0)
 
 
 def shifted(values, axis, offset):
@@ -221,7 +260,7 @@
         earlier, current = (current, fresh)
     lateral_smooth = smooth_lateral(correlation)
     reduced = reduce_shots(lateral_smooth, 1)
-    columns = lax.all_to_all(reduced, "depth", split_axis=1, concat_axis=0, tiled=True)
+    columns = proceed_the_inputs(reduced)
     gradient = smooth(columns, 0)
     return (earlier[0], current[0], earlier[1], current[1], gradient)
 

time: 130 us -> 133 us (1.023)
  blocking collectives: 14.1 us -> 0 us
  starting transfers between devices: 34.3 us -> 46.3 us
  waiting for transfers between devices: 30.9 us -> 36 us
    all_to_all x1 -> x0, blocking collectives: 14.1 us -> none  [on_device(): lax.all_to_all(reduced, 'depth', split_axis=1, concat_axis=0, tiled=True)]
    ppermute x0 -> x7, starting transfers between devices: none -> 12 us  [follow_side(): ppermute(current_arr, named_axis, perm=[(u, u ^ dev) for u in range(outer)])]
    ppermute x0 -> x7, waiting for transfers between devices: none -> 5.17 us  [follow_side(): ppermute(current_arr, named_axis, perm=[(u, u ^ dev) for u in range(outer)])]
    unnamed x54 -> x60, local copies, waits for them, and re-layouts: 5.44 us -> 4.64 us
  transfers between devices with their start and end apart: 12 -> 19, of which waited for: 4 -> 7; matrix products, arithmetic and copies ran while one was open for 31% -> 30% of each run, Pallas kernels for 0% -> 0%
where the time goes in v1:
time: 133 us; the launch traced here: 132 us
  starting transfers between devices  46.3 us (35%)
  waiting for transfers between devices  36 us (27%)
  matrix products  29.6 us (22%)
  local copies, waits for them, and re-layouts  13.8 us (10%)
  other arithmetic  5.02 us (4%)
  between operations  1.43 us (1%)
    ppermute x2, waiting for transfers between devices, on_device(): lax.ppermute(lax.slice_in_dim(fresh[i], length - 1, length, axis=zaxis),...  18.6 us
    dot_general x2, matrix products, spread_dense(): grid = jnp.dot(by_row, right, preferred_element_type=jnp.float32)  15 us
    ppermute x7, starting transfers between devices, follow_side(): ppermute(current_arr, named_axis, perm=[(u, u ^ dev) for u in range(outer)])  12 us
    ppermute x2, starting transfers between devices, exchange(): lax.ppermute(lax.slice_in_dim(f, length - HALO, length, axis=dim), 'depth...  11.1 us
    ppermute x2, starting transfers between devices, on_device(): lax.ppermute(lax.slice_in_dim(fresh[i], length - 1, length, axis=zaxis),...  9.35 us
    ppermute x2, waiting for transfers between devices, reduce_shots(): blocks = keep + lax.ppermute(send, 'shots', pairs)  8.68 us
    dot_general x4, matrix products, lateral_laplace(): along_x = jnp.einsum('...xy,kx->...ky', core, band(rows), precision=high)  7.45 us
    ppermute x2, starting transfers between devices, on_device(): lax.ppermute(lax.slice_in_dim(fresh[i], length - HALO, length - 1, axis=z...  6.76 us
  transfers between devices with their start and end apart: 19, of which 7 were waited for; matrix products, arithmetic and copies ran while one was open for 30% of the time, Pallas kernels for 0%

profile of v1, /device:TPU:0, one launch (start us, length us, event | category | flops | bytes accessed | tf_op | source)
XLA Modules:
  0.0 132.2 jit_solution(15307114353261218205)
XLA Ops:
  0.6 2.3 %fusion.275 = (f32[1,4,128,256]{3,2,1,0:T(8,128)}, f32[1,4,128,256]{3,2,1,0:T(8,128)}) fusion(f32[1,8,128,256]{3,2,1,0:T(8,128)} %param.13), kind=kLoop, calls=%fused_computation.364 | loop fusion | bytes 2097152 | tf_op jit(solution)/shard_map/slice | solution.py:126
  3.0 5.7 %collective-permute-start.1 = (f32[1,4,128,256]{3,2,1,0:T(8,128)}, f32[1,4,128,256]{3,2,1,0:T(8,128)}, u32[]{:S(2)}, u32[]{:S(2)}) collective-permute-start(f32[1,4,128,256]{3,2,1,0:T(8,128)} %get-tuple-element.30), channel_id=1, source_target_pairs={{0,1},{1,2},{2,3},{3,4},{4,5},{5,6},{6,7},{8,9},{9,10},{10,11},{11... | collective-permute-start | bytes 1572872 | tf_op jit(solution)/shard_map/ppermute | solution.py:124
  11.0 5.5 %collective-permute-start.3 = (f32[1,4,128,256]{3,2,1,0:T(8,128)}, f32[1,4,128,256]{3,2,1,0:T(8,128)}, u32[]{:S(2)}, u32[]{:S(2)}) collective-permute-start(f32[1,4,128,256]{3,2,1,0:T(8,128)} %get-tuple-element.28), channel_id=1, source_target_pairs={{0,1},{1,2},{2,3},{3,4},{4,5},{5,6},{6,7},{8,9},{9,10},{10,11},{11... | collective-permute-start | bytes 1572872 | tf_op jit(solution)/shard_map/ppermute | solution.py:124
  17.8 2.0 %convolution_bitcast_fusion.4 = f32[1,8,128,256]{3,2,1,0:T(8,128)} fusion(f32[1,8,128,256]{3,2,1,0:T(8,128)S(1)} %copy-done.5), kind=kOutput, calls=%fused_computation.34 | convolution fusion | flops 805961728 | bytes 2097152 | tf_op jit(solution)/shard_map/...xy,yk->...xk/dot_general | solution.py:76
  20.6 13.2 %fusion.1 = f32[1024,3,2,256]{3,0,2,1:T(8,128)S(1)} fusion(pred[4096,256]{0,1:T(8,128)(4,1)S(1)} %iota_compare_fusion.1, s32[4096]{0:T(1024)S(1)} %get-tuple-element.47, bf16[4096,3,2]{0,2,1:T(2,128)(2,1)S(1)} %maximum_bitcast_fusion), kind=kOutput, calls=%fused_computation.3 | convolution fusion | flops 12895387648 | bytes 7405568 | tf_op jit(solution)/shard_map/dot_general | solution.py:155
  35.7 1.8 %fusion.12 = f32[1024,3,2,256]{3,0,2,1:T(8,128)S(1)} fusion(pred[512,256]{0,1:T(8,128)(4,1)S(1)} %iota_compare_fusion.3, s32[512]{0:T(512)S(1)} %get-tuple-element.52, bf16[512,3,2]{0,2,1:T(2,128)(2,1)S(1)} %maximum_bitcast_fusion.1), kind=kOutput, calls=%fused_computation.22 | convolution fusion | flops 1611923456 | bytes 6430720 | tf_op jit(solution)/shard_map/dot_general | solution.py:155
  40.2 2.4 %fusion.26 = f32[1,8,128,256]{3,2,1,0:T(8,128)} fusion(f32[1,8,128,256]{3,2,1,0:T(8,128)S(1)} %bitcast.234, f32[1,8,128,256]{3,2,1,0:T(8,128)S(1)} %copy-done.9, f32[1,8,128,256]{3,2,1,0:T(8,128)S(1)} %copy-done.5, f32[8,128,256]{2,1,0:T(8,128)S(1)} %copy-done, f32[1,8,128,256]{3,2,1,0:T(8,128)S(1)} %copy-done.14), kind=kOutput, calls=%fused_computation.47 | convolution fusion | flops 404914176 | bytes 6291456 | tf_op jit(solution)/shard_map/...xy,kx->...ky/dot_general | solution.py:77
  43.8 2.4 %fusion.21 = f32[1,8,128,256]{3,2,1,0:T(8,128)} fusion(f32[1,8,128,256]{3,2,1,0:T(8,128)S(1)} %bitcast.235, f32[1,8,128,256]{3,2,1,0:T(8,128)S(1)} %convolution_bitcast_fusion.6, f32[1,8,128,256]{3,2,1,0:T(8,128)S(1)} %copy-done.3, f32[8,128,256]{2,1,0:T(8,128)S(1)} %copy-done, f32[1,8,128,256]{3,2,1,0:T(8,128)S(1)} %copy-done.15), kind=kOutput, calls=%fused_computation.42 | convolution fusion | flops 404914176 | bytes 6291456 | tf_op jit(solution)/shard_map/...xy,kx->...ky/dot_general | solution.py:77
  49.3 4.7 %collective-permute-start.2 = (f32[1,1,128,256]{3,2,1,0:T(8,128)S(1)}, f32[1,1,128,256]{3,2,1,0:T(8,128)S(1)}, u32[]{:S(2)}, u32[]{:S(2)}) collective-permute-start(f32[1,1,128,256]{3,2,1,0:T(8,128)S(1)} %slice.291), channel_id=1, source_target_pairs={{0,1},{1,2},{2,3},{3,4},{4,5},{5,6},{6,7},{8,9},{9,10},{10,11},{11... | collective-permute-start | bytes 393224 | tf_op jit(solution)/shard_map/ppermute | solution.py:238
  54.0 3.7 %collective-permute-start.7 = (f32[1,3,128,256]{3,2,1,0:T(8,128)S(1)}, f32[1,3,128,256]{3,2,1,0:T(8,128)S(1)}, u32[]{:S(2)}, u32[]{:S(2)}) collective-permute-start(f32[1,3,128,256]{3,2,1,0:T(8,128)S(1)} %slice.307), channel_id=1, source_target_pairs={{0,1},{1,2},{2,3},{3,4},{4,5},{5,6},{6,7},{8,9},{9,10},{10,11},{11... | collective-permute-start | bytes 1179656 | tf_op jit(solution)/shard_map/ppermute | solution.py:243
  63.1 4.7 %collective-permute-start.5 = (f32[1,1,128,256]{3,2,1,0:T(8,128)S(1)}, f32[1,1,128,256]{3,2,1,0:T(8,128)S(1)}, u32[]{:S(2)}, u32[]{:S(2)}) collective-permute-start(f32[1,1,128,256]{3,2,1,0:T(8,128)S(1)} %slice.300), channel_id=1, source_target_pairs={{0,1},{1,2},{2,3},{3,4},{4,5},{5,6},{6,7},{8,9},{9,10},{10,11},{11... | collective-permute-start | bytes 393224 | tf_op jit(solution)/shard_map/ppermute | solution.py:238
  69.3 3.1 %collective-permute-start.9 = (f32[1,3,128,256]{3,2,1,0:T(8,128)S(1)}, f32[1,3,128,256]{3,2,1,0:T(8,128)S(1)}, u32[]{:S(2)}, u32[]{:S(2)}) collective-permute-start(f32[1,3,128,256]{3,2,1,0:T(8,128)S(1)} %slice.316), channel_id=1, source_target_pairs={{0,1},{1,2},{2,3},{3,4},{4,5},{5,6},{6,7},{8,9},{9,10},{10,11},{11... | collective-permute-start | bytes 1179656 | tf_op jit(solution)/shard_map/ppermute | solution.py:243
  72.4 1.5 %collective-permute-start.8 = (f32[1,4,128,256]{3,2,1,0:T(8,128)S(1)}, f32[1,4,128,256]{3,2,1,0:T(8,128)S(1)}, u32[]{:S(2)}, u32[]{:S(2)}) collective-permute-start(f32[1,4,128,256]{3,2,1,0:T(8,128)S(1)} %slice.313), channel_id=1, source_target_pairs={{1,0},{2,1},{3,2},{4,3},{5,4},{6,5},{7,6},{9,8},{10,9},{11,10},{12... | collective-permute-start | bytes 1572872 | tf_op jit(solution)/shard_map/ppermute | solution.py:248
  73.9 18.6 %collective-permute-done.5 = f32[1,1,128,256]{3,2,1,0:T(8,128)S(1)} collective-permute-done((f32[1,1,128,256]{3,2,1,0:T(8,128)S(1)}, f32[1,1,128,256]{3,2,1,0:T(8,128)S(1)}, u32[]{:S(2)}, u32[]{:S(2)}) %collective-permute-start.5) | collective-permute-done | bytes 131104 | tf_op jit(solution)/shard_map/ppermute | solution.py:238
  95.1 3.5 %collective-permute-done.9 = f32[1,3,128,256]{3,2,1,0:T(8,128)S(1)} collective-permute-done((f32[1,3,128,256]{3,2,1,0:T(8,128)S(1)}, f32[1,3,128,256]{3,2,1,0:T(8,128)S(1)}, u32[]{:S(2)}, u32[]{:S(2)}) %collective-permute-start.9) | collective-permute-done | bytes 393248 | tf_op jit(solution)/shard_map/ppermute | solution.py:243
  102.5 1.9 %collective-permute-done.10 = f32[8,2,32,256]{3,2,1,0:T(8,128)S(1)} collective-permute-done((f32[8,2,32,256]{3,2,1,0:T(8,128)S(1)}, f32[8,2,32,256]{3,2,1,0:T(8,128)S(1)}, u32[]{:S(2)}, u32[]{:S(2)}) %collective-permute-start.10) | collective-permute-done | bytes 524320 | tf_op jit(solution)/shard_map/ppermute | solution.py:175
  104.5 1.6 %collective-permute-start.11 = (f32[8,1,32,256]{3,2,1,0:T(8,128)S(1)}, f32[8,1,32,256]{3,2,1,0:T(8,128)S(1)}, u32[]{:S(2)}, u32[]{:S(2)}) collective-permute-start(f32[8,1,32,256]{3,2,1,0:T(8,128)S(1)} %constant_dynamic-slice_fusion), channel_id=1, source_target_pairs={{0,16},{8,24},{16,0},{24,8},{1,17},{9,25},{17,1},{25,9},{2,18},{10... | collective-permute-start | bytes 786440 | tf_op jit(solution)/shard_map/ppermute | solution.py:175
  106.1 6.8 %collective-permute-done.11 = f32[8,1,32,256]{3,2,1,0:T(8,128)S(1)} collective-permute-done((f32[8,1,32,256]{3,2,1,0:T(8,128)S(1)}, f32[8,1,32,256]{3,2,1,0:T(8,128)S(1)}, u32[]{:S(2)}, u32[]{:S(2)}) %collective-permute-start.11) | collective-permute-done | bytes 262176 | tf_op jit(solution)/shard_map/ppermute | solution.py:175
  113.1 2.5 %collective-permute-start.12 = (f32[8,4,256]{2,1,0:T(4,128)S(1)}, f32[8,4,256]{2,1,0:T(4,128)S(1)}, u32[]{:S(2)}, u32[]{:S(2)}) collective-permute-start(f32[8,4,256]{2,1,0:T(4,128)S(1)} %get-tuple-element.43), channel_id=1, source_target_pairs={{0,1},{1,0},{2,3},{3,2},{4,5},{5,4},{6,7},{7,6},{8,9},{9,8},{10,11... | collective-permute-start | bytes 98312 | tf_op jit(solution)/shard_map/ppermute | solution.py:39
  117.2 2.8 %collective-permute-start.15 = (f32[8,4,256]{2,1,0:T(4,128)S(1)}, f32[8,4,256]{2,1,0:T(4,128)S(1)}, u32[]{:S(2)}, u32[]{:S(2)}) collective-permute-start(f32[8,4,256]{2,1,0:T(4,128)S(1)} %get-tuple-element.40), channel_id=1, source_target_pairs={{0,4},{1,5},{2,6},{3,7},{4,0},{5,1},{6,2},{7,3},{8,12},{9,13},{10,... | collective-permute-start | bytes 98312 | tf_op jit(solution)/shard_map/ppermute | solution.py:39
  120.0 1.5 %collective-permute-start.16 = (f32[8,4,256]{2,1,0:T(4,128)S(1)}, f32[8,4,256]{2,1,0:T(4,128)S(1)}, u32[]{:S(2)}, u32[]{:S(2)}) collective-permute-start(f32[8,4,256]{2,1,0:T(4,128)S(1)} %get-tuple-element.39), channel_id=1, source_target_pairs={{0,5},{1,4},{2,7},{3,6},{4,1},{5,0},{6,3},{7,2},{8,13},{9,12},{10,... | collective-permute-start | bytes 98312 | tf_op jit(solution)/shard_map/ppermute | solution.py:39
  121.5 2.2 %collective-permute-start.17 = (f32[8,4,256]{2,1,0:T(4,128)S(1)}, f32[8,4,256]{2,1,0:T(4,128)S(1)}, u32[]{:S(2)}, u32[]{:S(2)}) collective-permute-start(f32[8,4,256]{2,1,0:T(4,128)S(1)} %get-tuple-element.38), channel_id=1, source_target_pairs={{0,6},{1,7},{2,4},{3,5},{4,2},{5,3},{6,0},{7,1},{8,14},{9,15},{10,... | collective-permute-start | bytes 98312 | tf_op jit(solution)/shard_map/ppermute | solution.py:39
  125.7 1.5 %collective-permute-done.17 = f32[8,4,256]{2,1,0:T(4,128)S(1)} collective-permute-done((f32[8,4,256]{2,1,0:T(4,128)S(1)}, f32[8,4,256]{2,1,0:T(4,128)S(1)}, u32[]{:S(2)}, u32[]{:S(2)}) %collective-permute-start.17) | collective-permute-done | bytes 32800 | tf_op jit(solution)/shard_map/ppermute | solution.py:39
  127.3 3.1 %collective-permute-done.18 = f32[8,4,256]{2,1,0:T(4,128)S(1)} collective-permute-done((f32[8,4,256]{2,1,0:T(4,128)S(1)}, f32[8,4,256]{2,1,0:T(4,128)S(1)}, u32[]{:S(2)}, u32[]{:S(2)}) %collective-permute-start.18) | collective-permute-done | bytes 32800 | tf_op jit(solution)/shard_map/ppermute | solution.py:39
  (128 shorter events, 31.9 us)
Async XLA Ops:
  0.6 9.3 %copy-start.5 = (f32[1,8,128,256]{3,2,1,0:T(8,128)S(1)}, f32[1,8,128,256]{3,2,1,0:T(8,128)}, u32[]{:S(2)}) copy-start(f32[1,8,128,256]{3,2,1,0:T(8,128)} %param.15) | copy-start | bytes 3145732
  3.0 43.2 %collective-permute-start.1 = (f32[1,4,128,256]{3,2,1,0:T(8,128)}, f32[1,4,128,256]{3,2,1,0:T(8,128)}, u32[]{:S(2)}, u32[]{:S(2)}) collective-permute-start(f32[1,4,128,256]{3,2,1,0:T(8,128)} %get-tuple-element.30), channel_id=1, source_target_pairs={{0,1},{1,2},{2,3},{3,4},{4,5},{5,6},{6,7},{8,9},{9,10},{10,11},{11... | collective-permute-start | bytes 1572872 | tf_op jit(solution)/shard_map/ppermute | solution.py:124
  8.6 38.8 %collective-permute-start = (f32[1,4,128,256]{3,2,1,0:T(8,128)}, f32[1,4,128,256]{3,2,1,0:T(8,128)}, u32[]{:S(2)}, u32[]{:S(2)}) collective-permute-start(f32[1,4,128,256]{3,2,1,0:T(8,128)} %get-tuple-element.29), channel_id=1, source_target_pairs={{1,0},{2,1},{3,2},{4,3},{5,4},{6,5},{7,6},{9,8},{10,9},{11,10},{12... | collective-permute-start | bytes 1572872 | tf_op jit(solution)/shard_map/ppermute | solution.py:126
  11.0 49.0 %collective-permute-start.3 = (f32[1,4,128,256]{3,2,1,0:T(8,128)}, f32[1,4,128,256]{3,2,1,0:T(8,128)}, u32[]{:S(2)}, u32[]{:S(2)}) collective-permute-start(f32[1,4,128,256]{3,2,1,0:T(8,128)} %get-tuple-element.28), channel_id=1, source_target_pairs={{0,1},{1,2},{2,3},{3,4},{4,5},{5,6},{6,7},{8,9},{9,10},{10,11},{11... | collective-permute-start | bytes 1572872 | tf_op jit(solution)/shard_map/ppermute | solution.py:124
  16.5 43.6 %collective-permute-start.4 = (f32[1,4,128,256]{3,2,1,0:T(8,128)}, f32[1,4,128,256]{3,2,1,0:T(8,128)}, u32[]{:S(2)}, u32[]{:S(2)}) collective-permute-start(f32[1,4,128,256]{3,2,1,0:T(8,128)} %get-tuple-element.27), channel_id=1, source_target_pairs={{1,0},{2,1},{3,2},{4,3},{5,4},{6,5},{7,6},{9,8},{10,9},{11,10},{12... | collective-permute-start | bytes 1572872 | tf_op jit(solution)/shard_map/ppermute | solution.py:126
  49.2 50.7 %copy-start.2 = (f32[1,8,128,256]{3,2,1,0:T(8,128)}, f32[1,8,128,256]{3,2,1,0:T(8,128)S(1)}, u32[]{:S(2)}) copy-start(f32[1,8,128,256]{3,2,1,0:T(8,128)S(1)} %fusion.70) | copy-start | bytes 3145732
  49.3 11.9 %copy-start.6 = (f32[1,8,128,256]{3,2,1,0:T(8,128)S(1)}, f32[1,8,128,256]{3,2,1,0:T(8,128)}, u32[]{:S(2)}) copy-start(f32[1,8,128,256]{3,2,1,0:T(8,128)} %param.15) | copy-start | bytes 3145732
  49.3 10.8 %collective-permute-start.2 = (f32[1,1,128,256]{3,2,1,0:T(8,128)S(1)}, f32[1,1,128,256]{3,2,1,0:T(8,128)S(1)}, u32[]{:S(2)}, u32[]{:S(2)}) collective-permute-start(f32[1,1,128,256]{3,2,1,0:T(8,128)S(1)} %slice.291), channel_id=1, source_target_pairs={{0,1},{1,2},{2,3},{3,4},{4,5},{5,6},{6,7},{8,9},{9,10},{10,11},{11... | collective-permute-start | bytes 393224 | tf_op jit(solution)/shard_map/ppermute | solution.py:238
  54.0 40.9 %collective-permute-start.7 = (f32[1,3,128,256]{3,2,1,0:T(8,128)S(1)}, f32[1,3,128,256]{3,2,1,0:T(8,128)S(1)}, u32[]{:S(2)}, u32[]{:S(2)}) collective-permute-start(f32[1,3,128,256]{3,2,1,0:T(8,128)S(1)} %slice.307), channel_id=1, source_target_pairs={{0,1},{1,2},{2,3},{3,4},{4,5},{5,6},{6,7},{8,9},{9,10},{10,11},{11... | collective-permute-start | bytes 1179656 | tf_op jit(solution)/shard_map/ppermute | solution.py:243
  57.7 41.1 %collective-permute-start.6 = (f32[1,4,128,256]{3,2,1,0:T(8,128)S(1)}, f32[1,4,128,256]{3,2,1,0:T(8,128)S(1)}, u32[]{:S(2)}, u32[]{:S(2)}) collective-permute-start(f32[1,4,128,256]{3,2,1,0:T(8,128)S(1)} %slice.302), channel_id=1, source_target_pairs={{1,0},{2,1},{3,2},{4,3},{5,4},{6,5},{7,6},{9,8},{10,9},{11,10},{12... | collective-permute-start | bytes 1572872 | tf_op jit(solution)/shard_map/ppermute | solution.py:248
  63.1 36.7 %copy-start.1 = (f32[1,8,128,256]{3,2,1,0:T(8,128)}, f32[1,8,128,256]{3,2,1,0:T(8,128)S(1)}, u32[]{:S(2)}) copy-start(f32[1,8,128,256]{3,2,1,0:T(8,128)S(1)} %fusion.61) | copy-start | bytes 3145732
  63.1 29.4 %collective-permute-start.5 = (f32[1,1,128,256]{3,2,1,0:T(8,128)S(1)}, f32[1,1,128,256]{3,2,1,0:T(8,128)S(1)}, u32[]{:S(2)}, u32[]{:S(2)}) collective-permute-start(f32[1,1,128,256]{3,2,1,0:T(8,128)S(1)} %slice.300), channel_id=1, source_target_pairs={{0,1},{1,2},{2,3},{3,4},{4,5},{5,6},{6,7},{8,9},{9,10},{10,11},{11... | collective-permute-start | bytes 393224 | tf_op jit(solution)/shard_map/ppermute | solution.py:238
  69.3 24.3 %copy-start.10 = (f32[1,1024,256]{2,1,0:T(8,128)S(1)}, f32[1,1024,256]{2,1,0:T(8,128)}, u32[]{:S(2)}) copy-start(f32[1,1024,256]{2,1,0:T(8,128)} %get-tuple-element.19) | copy-start | bytes 3145732
  69.3 29.3 %collective-permute-start.9 = (f32[1,3,128,256]{3,2,1,0:T(8,128)S(1)}, f32[1,3,128,256]{3,2,1,0:T(8,128)S(1)}, u32[]{:S(2)}, u32[]{:S(2)}) collective-permute-start(f32[1,3,128,256]{3,2,1,0:T(8,128)S(1)} %slice.316), channel_id=1, source_target_pairs={{0,1},{1,2},{2,3},{3,4},{4,5},{5,6},{6,7},{8,9},{9,10},{10,11},{11... | collective-permute-start | bytes 1179656 | tf_op jit(solution)/shard_map/ppermute | solution.py:243
  72.4 26.9 %collective-permute-start.8 = (f32[1,4,128,256]{3,2,1,0:T(8,128)S(1)}, f32[1,4,128,256]{3,2,1,0:T(8,128)S(1)}, u32[]{:S(2)}, u32[]{:S(2)}) collective-permute-start(f32[1,4,128,256]{3,2,1,0:T(8,128)S(1)} %slice.313), channel_id=1, source_target_pairs={{1,0},{2,1},{3,2},{4,3},{5,4},{6,5},{7,6},{9,8},{10,9},{11,10},{12... | collective-permute-start | bytes 1572872 | tf_op jit(solution)/shard_map/ppermute | solution.py:248
  102.4 2.0 %collective-permute-start.10 = (f32[8,2,32,256]{3,2,1,0:T(8,128)S(1)}, f32[8,2,32,256]{3,2,1,0:T(8,128)S(1)}, u32[]{:S(2)}, u32[]{:S(2)}) collective-permute-start(f32[8,2,32,256]{3,2,1,0:T(8,128)S(1)} %dynamic-slice_bitcast_fusion), channel_id=1, source_target_pairs={{0,8},{8,0},{16,24},{24,16},{1,9},{9,1},{17,25},{25,17},{2,10},{10... | collective-permute-start | bytes 1572872 | tf_op jit(solution)/shard_map/ppermute | solution.py:175
  104.5 8.4 %collective-permute-start.11 = (f32[8,1,32,256]{3,2,1,0:T(8,128)S(1)}, f32[8,1,32,256]{3,2,1,0:T(8,128)S(1)}, u32[]{:S(2)}, u32[]{:S(2)}) collective-permute-start(f32[8,1,32,256]{3,2,1,0:T(8,128)S(1)} %constant_dynamic-slice_fusion), channel_id=1, source_target_pairs={{0,16},{8,24},{16,0},{24,8},{1,17},{9,25},{17,1},{25,9},{2,18},{10... | collective-permute-start | bytes 786440 | tf_op jit(solution)/shard_map/ppermute | solution.py:175
  113.1 8.4 %collective-permute-start.12 = (f32[8,4,256]{2,1,0:T(4,128)S(1)}, f32[8,4,256]{2,1,0:T(4,128)S(1)}, u32[]{:S(2)}, u32[]{:S(2)}) collective-permute-start(f32[8,4,256]{2,1,0:T(4,128)S(1)} %get-tuple-element.43), channel_id=1, source_target_pairs={{0,1},{1,0},{2,3},{3,2},{4,5},{5,4},{6,7},{7,6},{8,9},{9,8},{10,11... | collective-permute-start | bytes 98312 | tf_op jit(solution)/shard_map/ppermute | solution.py:39
  115.6 8.1 %collective-permute-start.13 = (f32[8,4,256]{2,1,0:T(4,128)S(1)}, f32[8,4,256]{2,1,0:T(4,128)S(1)}, u32[]{:S(2)}, u32[]{:S(2)}) collective-permute-start(f32[8,4,256]{2,1,0:T(4,128)S(1)} %get-tuple-element.42), channel_id=1, source_target_pairs={{0,2},{1,3},{2,0},{3,1},{4,6},{5,7},{6,4},{7,5},{8,10},{9,11},{10,... | collective-permute-start | bytes 98312 | tf_op jit(solution)/shard_map/ppermute | solution.py:39
  117.0 8.2 %collective-permute-start.14 = (f32[8,4,256]{2,1,0:T(4,128)S(1)}, f32[8,4,256]{2,1,0:T(4,128)S(1)}, u32[]{:S(2)}, u32[]{:S(2)}) collective-permute-start(f32[8,4,256]{2,1,0:T(4,128)S(1)} %get-tuple-element.41), channel_id=1, source_target_pairs={{0,3},{1,2},{2,1},{3,0},{4,7},{5,6},{6,5},{7,4},{8,11},{9,10},{10,... | collective-permute-start | bytes 98312 | tf_op jit(solution)/shard_map/ppermute | solution.py:39
  117.2 8.0 %collective-permute-start.15 = (f32[8,4,256]{2,1,0:T(4,128)S(1)}, f32[8,4,256]{2,1,0:T(4,128)S(1)}, u32[]{:S(2)}, u32[]{:S(2)}) collective-permute-start(f32[8,4,256]{2,1,0:T(4,128)S(1)} %get-tuple-element.40), channel_id=1, source_target_pairs={{0,4},{1,5},{2,6},{3,7},{4,0},{5,1},{6,2},{7,3},{8,12},{9,13},{10,... | collective-permute-start | bytes 98312 | tf_op jit(solution)/shard_map/ppermute | solution.py:39
  120.0 5.8 %collective-permute-start.16 = (f32[8,4,256]{2,1,0:T(4,128)S(1)}, f32[8,4,256]{2,1,0:T(4,128)S(1)}, u32[]{:S(2)}, u32[]{:S(2)}) collective-permute-start(f32[8,4,256]{2,1,0:T(4,128)S(1)} %get-tuple-element.39), channel_id=1, source_target_pairs={{0,5},{1,4},{2,7},{3,6},{4,1},{5,0},{6,3},{7,2},{8,13},{9,12},{10,... | collective-permute-start | bytes 98312 | tf_op jit(solution)/shard_map/ppermute | solution.py:39
  121.5 5.8 %collective-permute-start.17 = (f32[8,4,256]{2,1,0:T(4,128)S(1)}, f32[8,4,256]{2,1,0:T(4,128)S(1)}, u32[]{:S(2)}, u32[]{:S(2)}) collective-permute-start(f32[8,4,256]{2,1,0:T(4,128)S(1)} %get-tuple-element.38), channel_id=1, source_target_pairs={{0,6},{1,7},{2,4},{3,5},{4,2},{5,3},{6,0},{7,1},{8,14},{9,15},{10,... | collective-permute-start | bytes 98312 | tf_op jit(solution)/shard_map/ppermute | solution.py:39
  123.7 6.7 %collective-permute-start.18 = (f32[8,4,256]{2,1,0:T(4,128)S(1)}, f32[8,4,256]{2,1,0:T(4,128)S(1)}, u32[]{:S(2)}, u32[]{:S(2)}) collective-permute-start(f32[8,4,256]{2,1,0:T(4,128)S(1)} %get-tuple-element.37), channel_id=1, source_target_pairs={{0,7},{1,6},{2,5},{3,4},{4,3},{5,2},{6,1},{7,0},{8,15},{9,14},{10,... | collective-permute-start | bytes 98312 | tf_op jit(solution)/shard_map/ppermute | solution.py:39
  (18 other events, 49.7 us)
